TPU v7x, 32 devices: a whole 2x2x4 slice. The times are simulated.
32 devices in a mesh: gx: 4 (over y, x), gy: 8 (over z, core).
Axes of the slice: x: 2, y: 2, z: 4, core: 2. Of those that a mesh axis runs over, the one named last changes fastest.
Arguments:
- basis: float32 [4, 8, 3, 32, 192], P('gx', 'gy'), may hold values from -6 to 6
- coupling: bfloat16 [4, 8, 81, 192, 192], P('gx', 'gy'), as said below
- cpl_dst: int32 [4, 8, 81], P('gx', 'gy'), may hold values from 0 to 3, as said below
- cpl_src: int32 [4, 8, 81], P('gx', 'gy'), may hold values from 0 to 26, as said below
Outputs:
- subspace: float32 [4, 8, 3, 32, 192], P('gx', 'gy')
Inputs may be any that keep to these rules, and one draw needn't show every extreme that they name: `cpl_dst`: on each column the live slots come first; a live slot holds its target block's height 0 to 2, every later slot holds 3. The columns at gx index 0 have all 81 slots live. `cpl_src`: A live slot holds (3 dx + dy) * 3 + z for a source block in the column at offsets dx - 1, dy - 1 (periodic) and height z, within one height of the target block, periodically; each source block and column offset appears at most once per target; empty slots hold 0. `coupling`: the assembled matrix is symmetric: for every live slot that couples block i to block j there is a live slot on j's column that couples j to i and holds the transposed block.
All inputs are finite; a program needn't handle non-finite values.
Results may differ from a plain program's by a relative error of at most 0.0085.
Values may be sent and summed in bfloat16 or wider, within the bound.
No kernel may reach another device: no remote copies, remote signals or barrier semaphores. Data moves between devices by JAX's collectives and lax.ppermute only.
A program may use at most 64 MiB of HBM per device.

v0:
```python
import math
import jax
import jax.numpy as jnp
from jax import lax
from jax.sharding import PartitionSpec as P

DEGREE = 8
STEPS = 2
CENTER = 5.0
HALF = 3.0
LOWEST = 0.5


def with_halo(cells, sides, width):
    for axis, dim in sides:
        count = lax.axis_size(axis)
        head = lax.slice_in_dim(cells, 0, width, axis=dim)
        tail = lax.slice_in_dim(cells, cells.shape[dim] - width, cells.shape[dim], axis=dim)
        cells = jnp.concatenate(
            [
                lax.ppermute(tail, axis, [(i, (i + 1) % count) for i in range(count)]),
                cells,
                lax.ppermute(head, axis, [((i + 1) % count, i) for i in range(count)]),
            ],
            axis=dim,
        )
    return cells


def orthonormal(filtered, rows_total):
    local_block = filtered[0, 0]
    partial_gram = jnp.einsum(
        "zvd,zwd->vw", local_block, local_block, precision=lax.Precision.HIGHEST
    )
    gram_matrix = lax.psum(partial_gram, ("gx", "gy"))
    factor = jnp.linalg.cholesky(gram_matrix)
    identity = jnp.eye(local_block.shape[1], dtype=jnp.float32)
    inverse = jax.scipy.linalg.solve_triangular(factor, identity, lower=True)
    result = jnp.einsum("vw,zwd->zvd", inverse, local_block, precision=lax.Precision.HIGHEST)
    return (result * math.sqrt(rows_total))[None, None]


def local(basis, coupling, cpl_dst, cpl_src):
    column_depth = basis.shape[2]
    vector_count = basis.shape[3]
    block_rows = basis.shape[4]
    matrices = coupling[0, 0]
    targets = cpl_dst[0, 0]
    sources = cpl_src[0, 0]
    rows_total = lax.axis_size("gx") * lax.axis_size("gy") * column_depth * block_rows
    select = (targets[None, :] == jnp.arange(column_depth, dtype=jnp.int32)[:, None]).astype(
        jnp.float32
    )

    def apply_operator(current):
        rounded = current.astype(jnp.bfloat16)
        window = with_halo(rounded, (("gx", 0), ("gy", 1)), 1)
        window_cells = window.reshape(9 * column_depth, vector_count, block_rows)
        picked = jnp.take(window_cells, sources, axis=0)
        products = jnp.einsum("kvj,kij->kvi", picked, matrices, preferred_element_type=jnp.float32)
        applied = jnp.einsum("zk,kvi->zvi", select, products, precision=lax.Precision.HIGHEST)
        return applied[None, None]

    sigma_one = HALF / (LOWEST - CENTER)
    current_basis = basis
    for outer in range(STEPS):
        previous = current_basis
        current = sigma_one / HALF * (apply_operator(previous) - CENTER * previous)
        sigma_now = sigma_one
        for inner in range(1, DEGREE):
            sigma_next = 1.0 / (2.0 / sigma_one - sigma_now)
            image = apply_operator(current)
            following = (
                2.0 * sigma_next / HALF * (image - CENTER * current)
                - sigma_now * sigma_next * previous
            )
            previous, current, sigma_now = (current, following, sigma_next)
        current_basis = orthonormal(current, rows_total)
    return current_basis


def solution(mesh):
    placed = (
        P("gx", "gy", None, None, None),
        P("gx", "gy", None, None, None),
        P("gx", "gy", None),
        P("gx", "gy", None),
    )
    return jax.shard_map(
        local,
        mesh=mesh,
        in_specs=placed,
        out_specs=P("gx", "gy", None, None, None),
        check_vma=False,
    )
```

profile of v0, /device:TPU:0, one launch (start us, length us, event | category | flops | bytes accessed | tf_op | source)
XLA Modules:
  0.0 457.4 jit_solution(3541501361220826311)
XLA Ops:
  0.9 3.9 collective-permute-start.1
  6.5 3.2 collective-permute-done
  11.5 3.7 collective-permute-done.3
  15.2 3.0 collective-permute-done.2
  19.0 5.8 %fusion.30 = f32[81,32,192]{2,1,0:T(8,128)S(1)} fusion(bf16[1,1,81,192,192]{4,3,2,1,0:T(8,128)(2,1)} %param.10, bf16[81,32,192]{2,1,0:T(8,128)(2,1)S(1)} %gather_fusion, pred[81]{0:T(512)(128)(4,1)S(1)} %compare_and_fusion), kind=kOutput, calls=%fused_computation.46 | convolution fusion | flops 191600640 | bytes 8958033 | tf_op jit(solution)/shard_map/kvj,kij->kvi/dot_general | solution.py:60
  24.9 2.6 multiply_convert_fusion
  33.4 4.6 %collective-permute-done.7 = bf16[3,1,3,32,192]{4,2,3,1,0:T(4,128)(2,1)S(1)} collective-permute-done((bf16[3,1,3,32,192]{4,2,3,1,0:T(4,128)(2,1)S(1)}, bf16[3,1,3,32,192]{4,2,3,1,0:T(4,128)(2,1)S(1)}, u32[]{:S(2)}, u32[]{:S(2)}) %collective-permute-start.7) | collective-permute-done | bytes 110624 | tf_op jit(solution)/shard_map/ppermute | solution.py:23
  41.6 5.8 %fusion.28 = f32[81,32,192]{2,1,0:T(8,128)S(1)} fusion(bf16[1,1,81,192,192]{4,3,2,1,0:T(8,128)(2,1)} %param.10, bf16[81,32,192]{2,1,0:T(8,128)(2,1)S(1)} %gather_fusion.1, pred[81]{0:T(512)(128)(4,1)S(1)} %compare_and_fusion), kind=kOutput, calls=%fused_computation.44 | convolution fusion | flops 191600640 | bytes 8958033 | tf_op jit(solution)/shard_map/kvj,kij->kvi/dot_general | solution.py:60
  47.4 2.6 fusion.269
  57.8 3.8 collective-permute-done.11
  61.6 3.1 collective-permute-done.10
  66.1 5.8 %fusion.26 = f32[81,32,192]{2,1,0:T(8,128)S(1)} fusion(bf16[1,1,81,192,192]{4,3,2,1,0:T(8,128)(2,1)} %param.10, bf16[81,32,192]{2,1,0:T(8,128)(2,1)S(1)} %gather_fusion.2, pred[81]{0:T(512)(128)(4,1)S(1)} %compare_and_fusion), kind=kOutput, calls=%fused_computation.42 | convolution fusion | flops 191600640 | bytes 8958033 | tf_op jit(solution)/shard_map/kvj,kij->kvi/dot_general | solution.py:60
  71.9 2.5 fusion.270
  81.3 4.6 %collective-permute-done.15 = bf16[3,1,3,32,192]{4,2,3,1,0:T(4,128)(2,1)S(1)} collective-permute-done((bf16[3,1,3,32,192]{4,2,3,1,0:T(4,128)(2,1)S(1)}, bf16[3,1,3,32,192]{4,2,3,1,0:T(4,128)(2,1)S(1)}, u32[]{:S(2)}, u32[]{:S(2)}) %collective-permute-start.15) | collective-permute-done | bytes 110624 | tf_op jit(solution)/shard_map/ppermute | solution.py:23
  89.1 5.8 %fusion.24 = f32[81,32,192]{2,1,0:T(8,128)S(1)} fusion(bf16[1,1,81,192,192]{4,3,2,1,0:T(8,128)(2,1)} %param.10, bf16[81,32,192]{2,1,0:T(8,128)(2,1)S(1)} %gather_fusion.3, pred[81]{0:T(512)(128)(4,1)S(1)} %compare_and_fusion), kind=kOutput, calls=%fused_computation.40 | convolution fusion | flops 191600640 | bytes 8958033 | tf_op jit(solution)/shard_map/kvj,kij->kvi/dot_general | solution.py:60
  94.9 2.5 fusion.271
  104.5 4.8 %collective-permute-done.19 = bf16[3,1,3,32,192]{4,2,3,1,0:T(4,128)(2,1)S(1)} collective-permute-done((bf16[3,1,3,32,192]{4,2,3,1,0:T(4,128)(2,1)S(1)}, bf16[3,1,3,32,192]{4,2,3,1,0:T(4,128)(2,1)S(1)}, u32[]{:S(2)}, u32[]{:S(2)}) %collective-permute-start.19) | collective-permute-done | bytes 110624 | tf_op jit(solution)/shard_map/ppermute | solution.py:23
  112.7 5.8 %fusion.22 = f32[81,32,192]{2,1,0:T(8,128)S(1)} fusion(bf16[1,1,81,192,192]{4,3,2,1,0:T(8,128)(2,1)} %param.10, bf16[81,32,192]{2,1,0:T(8,128)(2,1)S(1)} %gather_fusion.4, pred[81]{0:T(512)(128)(4,1)S(1)} %compare_and_fusion), kind=kOutput, calls=%fused_computation.38 | convolution fusion | flops 191600640 | bytes 8958033 | tf_op jit(solution)/shard_map/kvj,kij->kvi/dot_general | solution.py:60
  118.5 2.5 fusion.272
  127.5 4.6 %collective-permute-done.23 = bf16[3,1,3,32,192]{4,2,3,1,0:T(4,128)(2,1)S(1)} collective-permute-done((bf16[3,1,3,32,192]{4,2,3,1,0:T(4,128)(2,1)S(1)}, bf16[3,1,3,32,192]{4,2,3,1,0:T(4,128)(2,1)S(1)}, u32[]{:S(2)}, u32[]{:S(2)}) %collective-permute-start.23) | collective-permute-done | bytes 110624 | tf_op jit(solution)/shard_map/ppermute | solution.py:23
  135.3 5.8 %fusion.20 = f32[81,32,192]{2,1,0:T(8,128)S(1)} fusion(bf16[1,1,81,192,192]{4,3,2,1,0:T(8,128)(2,1)} %param.10, bf16[81,32,192]{2,1,0:T(8,128)(2,1)S(1)} %gather_fusion.5, pred[81]{0:T(512)(128)(4,1)S(1)} %compare_and_fusion), kind=kOutput, calls=%fused_computation.36 | convolution fusion | flops 191600640 | bytes 8958033 | tf_op jit(solution)/shard_map/kvj,kij->kvi/dot_general | solution.py:60
  150.9 4.6 %collective-permute-done.27 = bf16[3,1,3,32,192]{4,2,3,1,0:T(4,128)(2,1)S(1)} collective-permute-done((bf16[3,1,3,32,192]{4,2,3,1,0:T(4,128)(2,1)S(1)}, bf16[3,1,3,32,192]{4,2,3,1,0:T(4,128)(2,1)S(1)}, u32[]{:S(2)}, u32[]{:S(2)}) %collective-permute-start.27) | collective-permute-done | bytes 110624 | tf_op jit(solution)/shard_map/ppermute | solution.py:23
  159.1 5.8 %fusion.18 = f32[81,32,192]{2,1,0:T(8,128)S(1)} fusion(bf16[1,1,81,192,192]{4,3,2,1,0:T(8,128)(2,1)} %param.10, bf16[81,32,192]{2,1,0:T(8,128)(2,1)S(1)} %gather_fusion.6, pred[81]{0:T(512)(128)(4,1)S(1)} %compare_and_fusion), kind=kOutput, calls=%fused_computation.34 | convolution fusion | flops 191600640 | bytes 8958033 | tf_op jit(solution)/shard_map/kvj,kij->kvi/dot_general | solution.py:60
  164.9 2.5 fusion.274
  174.5 4.6 %collective-permute-done.31 = bf16[3,1,3,32,192]{4,2,3,1,0:T(4,128)(2,1)S(1)} collective-permute-done((bf16[3,1,3,32,192]{4,2,3,1,0:T(4,128)(2,1)S(1)}, bf16[3,1,3,32,192]{4,2,3,1,0:T(4,128)(2,1)S(1)}, u32[]{:S(2)}, u32[]{:S(2)}) %collective-permute-start.31) | collective-permute-done | bytes 110624 | tf_op jit(solution)/shard_map/ppermute | solution.py:23
  182.4 5.8 %fusion.16 = f32[81,32,192]{2,1,0:T(8,128)S(1)} fusion(bf16[1,1,81,192,192]{4,3,2,1,0:T(8,128)(2,1)} %param.10, bf16[81,32,192]{2,1,0:T(8,128)(2,1)S(1)} %gather_fusion.7, pred[81]{0:T(512)(128)(4,1)S(1)} %compare_and_fusion), kind=kOutput, calls=%fused_computation.32 | convolution fusion | flops 191600640 | bytes 8958033 | tf_op jit(solution)/shard_map/kvj,kij->kvi/dot_general | solution.py:60
  191.0 38.2 %psum.14 = f32[32,32]{0,1:T(8,128)S(1)} all-reduce(f32[32,32]{0,1:T(8,128)S(1)} %convolution_bitcast_fusion.3), channel_id=1, replica_groups=mesh['gx'=4,'gy'=8] {'gx','gy'}, use_global_device_ids=true, to_apply=%region_0.0 | all-reduce | flops 1024 | bytes 8192 | tf_op jit(solution)/shard_map/psum | solution.py:35
  229.2 2.9 cholesky.44
  241.2 2.6 collective-permute-done.32
  246.8 3.7 collective-permute-done.34
  251.2 5.8 %fusion.14 = f32[81,32,192]{2,1,0:T(8,128)S(1)} fusion(bf16[1,1,81,192,192]{4,3,2,1,0:T(8,128)(2,1)} %param.10, bf16[81,32,192]{2,1,0:T(8,128)(2,1)S(1)} %gather_fusion.8, pred[81]{0:T(512)(128)(4,1)S(1)} %compare_and_fusion), kind=kOutput, calls=%fused_computation.30 | convolution fusion | flops 191600640 | bytes 8958033 | tf_op jit(solution)/shard_map/kvj,kij->kvi/dot_general | solution.py:60
  265.8 3.7 collective-permute-done.39
  272.5 5.8 %fusion.12 = f32[81,32,192]{2,1,0:T(8,128)S(1)} fusion(bf16[1,1,81,192,192]{4,3,2,1,0:T(8,128)(2,1)} %param.10, bf16[81,32,192]{2,1,0:T(8,128)(2,1)S(1)} %gather_fusion.9, pred[81]{0:T(512)(128)(4,1)S(1)} %compare_and_fusion), kind=kOutput, calls=%fused_computation.28 | convolution fusion | flops 191600640 | bytes 8958033 | tf_op jit(solution)/shard_map/kvj,kij->kvi/dot_general | solution.py:60
  288.2 3.6 collective-permute-done.43
  295.0 5.8 %fusion.10 = f32[81,32,192]{2,1,0:T(8,128)S(1)} fusion(bf16[1,1,81,192,192]{4,3,2,1,0:T(8,128)(2,1)} %param.10, bf16[81,32,192]{2,1,0:T(8,128)(2,1)S(1)} %gather_fusion.10, pred[81]{0:T(512)(128)(4,1)S(1)} %compare_and_fusion), kind=kOutput, calls=%fused_computation.26 | convolution fusion | flops 191600640 | bytes 8958033 | tf_op jit(solution)/shard_map/kvj,kij->kvi/dot_general | solution.py:60
  309.6 3.6 collective-permute-done.47
  316.3 5.8 %fusion.8 = f32[81,32,192]{2,1,0:T(8,128)S(1)} fusion(bf16[1,1,81,192,192]{4,3,2,1,0:T(8,128)(2,1)} %param.10, bf16[81,32,192]{2,1,0:T(8,128)(2,1)S(1)} %gather_fusion.11, pred[81]{0:T(512)(128)(4,1)S(1)} %compare_and_fusion), kind=kOutput, calls=%fused_computation.24 | convolution fusion | flops 191600640 | bytes 8958033 | tf_op jit(solution)/shard_map/kvj,kij->kvi/dot_general | solution.py:60
  331.3 3.1 collective-permute-done.51
  334.5 2.8 collective-permute-done.50
  338.0 5.8 %fusion.6 = f32[81,32,192]{2,1,0:T(8,128)S(1)} fusion(bf16[1,1,81,192,192]{4,3,2,1,0:T(8,128)(2,1)} %param.10, bf16[81,32,192]{2,1,0:T(8,128)(2,1)S(1)} %gather_fusion.12, pred[81]{0:T(512)(128)(4,1)S(1)} %compare_and_fusion), kind=kOutput, calls=%fused_computation.22 | convolution fusion | flops 191600640 | bytes 8958033 | tf_op jit(solution)/shard_map/kvj,kij->kvi/dot_general | solution.py:60
  353.1 3.6 collective-permute-done.55
  359.8 5.8 %fusion.4 = f32[81,32,192]{2,1,0:T(8,128)S(1)} fusion(bf16[1,1,81,192,192]{4,3,2,1,0:T(8,128)(2,1)} %param.10, bf16[81,32,192]{2,1,0:T(8,128)(2,1)S(1)} %gather_fusion.13, pred[81]{0:T(512)(128)(4,1)S(1)} %compare_and_fusion), kind=kOutput, calls=%fused_computation.20 | convolution fusion | flops 191600640 | bytes 8958033 | tf_op jit(solution)/shard_map/kvj,kij->kvi/dot_general | solution.py:60
  374.9 3.6 collective-permute-done.59
  381.7 5.8 %fusion.2 = f32[81,32,192]{2,1,0:T(8,128)S(1)} fusion(bf16[1,1,81,192,192]{4,3,2,1,0:T(8,128)(2,1)} %param.10, bf16[81,32,192]{2,1,0:T(8,128)(2,1)S(1)} %gather_fusion.14, pred[81]{0:T(512)(128)(4,1)S(1)} %compare_and_fusion), kind=kOutput, calls=%fused_computation.18 | convolution fusion | flops 191600640 | bytes 8958033 | tf_op jit(solution)/shard_map/kvj,kij->kvi/dot_general | solution.py:60
  396.3 3.6 collective-permute-done.63
  403.0 5.8 %fusion = f32[81,32,192]{2,1,0:T(8,128)S(1)} fusion(bf16[1,1,81,192,192]{4,3,2,1,0:T(8,128)(2,1)} %param.10, bf16[81,32,192]{2,1,0:T(8,128)(2,1)S(1)} %gather_fusion.15, pred[81]{0:T(512)(128)(4,1)S(1)} %compare_and_fusion), kind=kOutput, calls=%fused_computation.16 | convolution fusion | flops 191600640 | bytes 8958033 | tf_op jit(solution)/shard_map/kvj,kij->kvi/dot_general | solution.py:60
  411.6 37.7 %psum.15 = f32[32,32]{0,1:T(8,128)S(1)} all-reduce(f32[32,32]{0,1:T(8,128)S(1)} %convolution_bitcast_fusion.1), channel_id=1, replica_groups=mesh['gx'=4,'gy'=8] {'gx','gy'}, use_global_device_ids=true, to_apply=%region_3.7 | all-reduce | flops 1024 | bytes 8192 | tf_op jit(solution)/shard_map/psum | solution.py:35
  449.4 2.9 cholesky.55
  (206 shorter events, 184.4 us)
Async XLA Ops:
  0.9 5.6 %collective-permute-start.1 = (bf16[1,1,3,32,192]{4,3,2,1,0:T(8,128)(2,1)S(1)}, bf16[1,1,3,32,192]{4,3,2,1,0:T(8,128)(2,1)S(1)}, u32[]{:S(2)}, u32[]{:S(2)}) collective-permute-start(bf16[1,1,3,32,192]{4,3,2,1,0:T(8,128)(2,1)S(1)} %convert_element_type.82), channel_id=1, source_target_pairs={{8,0},{16,8},{24,16},{0,24},{9,1},{17,9},{25,17},{1,25},{10,2},{18... | collective-permute-start | bytes 110600 | tf_op jit(solution)/shard_map/ppermute | solution.py:23
  4.8 5.0 %collective-permute-start = (bf16[1,1,3,32,192]{4,3,2,1,0:T(8,128)(2,1)S(1)}, bf16[1,1,3,32,192]{4,3,2,1,0:T(8,128)(2,1)S(1)}, u32[]{:S(2)}, u32[]{:S(2)}) collective-permute-start(bf16[1,1,3,32,192]{4,3,2,1,0:T(8,128)(2,1)S(1)} %convert_element_type.82), channel_id=1, source_target_pairs={{0,8},{8,16},{16,24},{24,0},{1,9},{9,17},{17,25},{25,1},{2,10},{10... | collective-permute-start | bytes 110600 | tf_op jit(solution)/shard_map/ppermute | solution.py:21
  9.8 5.4 %collective-permute-start.3 = (bf16[3,1,3,32,192]{4,3,2,1,0:T(8,128)(2,1)S(1)}, bf16[3,1,3,32,192]{4,3,2,1,0:T(8,128)(2,1)S(1)}, u32[]{:S(2)}, u32[]{:S(2)}) collective-permute-start(bf16[3,1,3,32,192]{4,3,2,1,0:T(8,128)(2,1)S(1)} %pad_maximum_fusion.23), channel_id=1, source_target_pairs={{1,0},{2,1},{3,2},{4,3},{5,4},{6,5},{7,6},{0,7},{9,8},{10,9},{11,1... | collective-permute-start | bytes 331784 | tf_op jit(solution)/shard_map/ppermute | solution.py:23
  11.5 6.7 %collective-permute-start.2 = (bf16[3,1,3,32,192]{4,3,2,1,0:T(8,128)(2,1)S(1)}, bf16[3,1,3,32,192]{4,3,2,1,0:T(8,128)(2,1)S(1)}, u32[]{:S(2)}, u32[]{:S(2)}) collective-permute-start(bf16[3,1,3,32,192]{4,3,2,1,0:T(8,128)(2,1)S(1)} %pad_maximum_fusion.23), channel_id=1, source_target_pairs={{0,1},{1,2},{2,3},{3,4},{4,5},{5,6},{6,7},{7,0},{8,9},{9,10},{10,1... | collective-permute-start | bytes 331784 | tf_op jit(solution)/shard_map/ppermute | solution.py:21
  27.4 4.3 collective-permute-start.5
  27.5 5.2 %collective-permute-start.4 = (bf16[1,1,3,32,192]{4,2,3,1,0:T(4,128)(2,1)S(1)}, bf16[1,1,3,32,192]{4,2,3,1,0:T(4,128)(2,1)S(1)}, u32[]{:S(2)}, u32[]{:S(2)}) collective-permute-start(bf16[1,1,3,32,192]{4,2,3,1,0:T(4,128)(2,1)S(1)} %get-tuple-element.18), channel_id=1, source_target_pairs={{0,8},{8,16},{16,24},{24,0},{1,9},{9,17},{17,25},{25,1},{2,10},{10... | collective-permute-start | bytes 110600 | tf_op jit(solution)/shard_map/ppermute | solution.py:21
  32.9 5.2 %collective-permute-start.7 = (bf16[3,1,3,32,192]{4,2,3,1,0:T(4,128)(2,1)S(1)}, bf16[3,1,3,32,192]{4,2,3,1,0:T(4,128)(2,1)S(1)}, u32[]{:S(2)}, u32[]{:S(2)}) collective-permute-start(bf16[3,1,3,32,192]{4,2,3,1,0:T(4,128)(2,1)S(1)} %pad_maximum_fusion.16), channel_id=1, source_target_pairs={{1,0},{2,1},{3,2},{4,3},{5,4},{6,5},{7,6},{0,7},{9,8},{10,9},{11,1... | collective-permute-start | bytes 331784 | tf_op jit(solution)/shard_map/ppermute | solution.py:23
  32.9 7.3 %collective-permute-start.6 = (bf16[3,1,3,32,192]{4,2,3,1,0:T(4,128)(2,1)S(1)}, bf16[3,1,3,32,192]{4,2,3,1,0:T(4,128)(2,1)S(1)}, u32[]{:S(2)}, u32[]{:S(2)}) collective-permute-start(bf16[3,1,3,32,192]{4,2,3,1,0:T(4,128)(2,1)S(1)} %pad_maximum_fusion.16), channel_id=1, source_target_pairs={{0,1},{1,2},{2,3},{3,4},{4,5},{5,6},{6,7},{7,0},{8,9},{9,10},{10,1... | collective-permute-start | bytes 331784 | tf_op jit(solution)/shard_map/ppermute | solution.py:21
  50.0 4.3 collective-permute-start.9
  50.9 5.2 %collective-permute-start.8 = (bf16[1,1,3,32,192]{4,2,3,1,0:T(4,128)(2,1)S(1)}, bf16[1,1,3,32,192]{4,2,3,1,0:T(4,128)(2,1)S(1)}, u32[]{:S(2)}, u32[]{:S(2)}) collective-permute-start(bf16[1,1,3,32,192]{4,2,3,1,0:T(4,128)(2,1)S(1)} %get-tuple-element.20), channel_id=1, source_target_pairs={{0,8},{8,16},{16,24},{24,0},{1,9},{9,17},{17,25},{25,1},{2,10},{10... | collective-permute-start | bytes 110600 | tf_op jit(solution)/shard_map/ppermute | solution.py:21
  56.3 5.3 %collective-permute-start.11 = (bf16[3,1,3,32,192]{4,2,3,1,0:T(4,128)(2,1)S(1)}, bf16[3,1,3,32,192]{4,2,3,1,0:T(4,128)(2,1)S(1)}, u32[]{:S(2)}, u32[]{:S(2)}) collective-permute-start(bf16[3,1,3,32,192]{4,2,3,1,0:T(4,128)(2,1)S(1)} %pad_maximum_fusion.17), channel_id=1, source_target_pairs={{1,0},{2,1},{3,2},{4,3},{5,4},{6,5},{7,6},{0,7},{9,8},{10,9},{11,1... | collective-permute-start | bytes 331784 | tf_op jit(solution)/shard_map/ppermute | solution.py:23
  57.7 7.0 %collective-permute-start.10 = (bf16[3,1,3,32,192]{4,2,3,1,0:T(4,128)(2,1)S(1)}, bf16[3,1,3,32,192]{4,2,3,1,0:T(4,128)(2,1)S(1)}, u32[]{:S(2)}, u32[]{:S(2)}) collective-permute-start(bf16[3,1,3,32,192]{4,2,3,1,0:T(4,128)(2,1)S(1)} %pad_maximum_fusion.17), channel_id=1, source_target_pairs={{0,1},{1,2},{2,3},{3,4},{4,5},{5,6},{6,7},{7,0},{8,9},{9,10},{10,1... | collective-permute-start | bytes 331784 | tf_op jit(solution)/shard_map/ppermute | solution.py:21
  74.4 4.3 collective-permute-start.13
  75.4 5.2 %collective-permute-start.12 = (bf16[1,1,3,32,192]{4,2,3,1,0:T(4,128)(2,1)S(1)}, bf16[1,1,3,32,192]{4,2,3,1,0:T(4,128)(2,1)S(1)}, u32[]{:S(2)}, u32[]{:S(2)}) collective-permute-start(bf16[1,1,3,32,192]{4,2,3,1,0:T(4,128)(2,1)S(1)} %get-tuple-element.22), channel_id=1, source_target_pairs={{0,8},{8,16},{16,24},{24,0},{1,9},{9,17},{17,25},{25,1},{2,10},{10... | collective-permute-start | bytes 110600 | tf_op jit(solution)/shard_map/ppermute | solution.py:21
  80.8 5.2 %collective-permute-start.15 = (bf16[3,1,3,32,192]{4,2,3,1,0:T(4,128)(2,1)S(1)}, bf16[3,1,3,32,192]{4,2,3,1,0:T(4,128)(2,1)S(1)}, u32[]{:S(2)}, u32[]{:S(2)}) collective-permute-start(bf16[3,1,3,32,192]{4,2,3,1,0:T(4,128)(2,1)S(1)} %pad_maximum_fusion.18), channel_id=1, source_target_pairs={{1,0},{2,1},{3,2},{4,3},{5,4},{6,5},{7,6},{0,7},{9,8},{10,9},{11,1... | collective-permute-start | bytes 331784 | tf_op jit(solution)/shard_map/ppermute | solution.py:23
  80.8 6.9 %collective-permute-start.14 = (bf16[3,1,3,32,192]{4,2,3,1,0:T(4,128)(2,1)S(1)}, bf16[3,1,3,32,192]{4,2,3,1,0:T(4,128)(2,1)S(1)}, u32[]{:S(2)}, u32[]{:S(2)}) collective-permute-start(bf16[3,1,3,32,192]{4,2,3,1,0:T(4,128)(2,1)S(1)} %pad_maximum_fusion.18), channel_id=1, source_target_pairs={{0,1},{1,2},{2,3},{3,4},{4,5},{5,6},{6,7},{7,0},{8,9},{9,10},{10,1... | collective-permute-start | bytes 331784 | tf_op jit(solution)/shard_map/ppermute | solution.py:21
  97.5 4.3 collective-permute-start.17
  98.4 5.2 %collective-permute-start.16 = (bf16[1,1,3,32,192]{4,2,3,1,0:T(4,128)(2,1)S(1)}, bf16[1,1,3,32,192]{4,2,3,1,0:T(4,128)(2,1)S(1)}, u32[]{:S(2)}, u32[]{:S(2)}) collective-permute-start(bf16[1,1,3,32,192]{4,2,3,1,0:T(4,128)(2,1)S(1)} %get-tuple-element.24), channel_id=1, source_target_pairs={{0,8},{8,16},{16,24},{24,0},{1,9},{9,17},{17,25},{25,1},{2,10},{10... | collective-permute-start | bytes 110600 | tf_op jit(solution)/shard_map/ppermute | solution.py:21
  103.8 5.5 %collective-permute-start.19 = (bf16[3,1,3,32,192]{4,2,3,1,0:T(4,128)(2,1)S(1)}, bf16[3,1,3,32,192]{4,2,3,1,0:T(4,128)(2,1)S(1)}, u32[]{:S(2)}, u32[]{:S(2)}) collective-permute-start(bf16[3,1,3,32,192]{4,2,3,1,0:T(4,128)(2,1)S(1)} %pad_maximum_fusion.19), channel_id=1, source_target_pairs={{1,0},{2,1},{3,2},{4,3},{5,4},{6,5},{7,6},{0,7},{9,8},{10,9},{11,1... | collective-permute-start | bytes 331784 | tf_op jit(solution)/shard_map/ppermute | solution.py:23
  104.2 7.1 %collective-permute-start.18 = (bf16[3,1,3,32,192]{4,2,3,1,0:T(4,128)(2,1)S(1)}, bf16[3,1,3,32,192]{4,2,3,1,0:T(4,128)(2,1)S(1)}, u32[]{:S(2)}, u32[]{:S(2)}) collective-permute-start(bf16[3,1,3,32,192]{4,2,3,1,0:T(4,128)(2,1)S(1)} %pad_maximum_fusion.19), channel_id=1, source_target_pairs={{0,1},{1,2},{2,3},{3,4},{4,5},{5,6},{6,7},{7,0},{8,9},{9,10},{10,1... | collective-permute-start | bytes 331784 | tf_op jit(solution)/shard_map/ppermute | solution.py:21
  121.0 4.3 collective-permute-start.21
  121.6 5.2 %collective-permute-start.20 = (bf16[1,1,3,32,192]{4,2,3,1,0:T(4,128)(2,1)S(1)}, bf16[1,1,3,32,192]{4,2,3,1,0:T(4,128)(2,1)S(1)}, u32[]{:S(2)}, u32[]{:S(2)}) collective-permute-start(bf16[1,1,3,32,192]{4,2,3,1,0:T(4,128)(2,1)S(1)} %get-tuple-element.26), channel_id=1, source_target_pairs={{0,8},{8,16},{16,24},{24,0},{1,9},{9,17},{17,25},{25,1},{2,10},{10... | collective-permute-start | bytes 110600 | tf_op jit(solution)/shard_map/ppermute | solution.py:21
  127.0 5.2 %collective-permute-start.23 = (bf16[3,1,3,32,192]{4,2,3,1,0:T(4,128)(2,1)S(1)}, bf16[3,1,3,32,192]{4,2,3,1,0:T(4,128)(2,1)S(1)}, u32[]{:S(2)}, u32[]{:S(2)}) collective-permute-start(bf16[3,1,3,32,192]{4,2,3,1,0:T(4,128)(2,1)S(1)} %pad_maximum_fusion.20), channel_id=1, source_target_pairs={{1,0},{2,1},{3,2},{4,3},{5,4},{6,5},{7,6},{0,7},{9,8},{10,9},{11,1... | collective-permute-start | bytes 331784 | tf_op jit(solution)/shard_map/ppermute | solution.py:23
  127.0 6.9 %collective-permute-start.22 = (bf16[3,1,3,32,192]{4,2,3,1,0:T(4,128)(2,1)S(1)}, bf16[3,1,3,32,192]{4,2,3,1,0:T(4,128)(2,1)S(1)}, u32[]{:S(2)}, u32[]{:S(2)}) collective-permute-start(bf16[3,1,3,32,192]{4,2,3,1,0:T(4,128)(2,1)S(1)} %pad_maximum_fusion.20), channel_id=1, source_target_pairs={{0,1},{1,2},{2,3},{3,4},{4,5},{5,6},{6,7},{7,0},{8,9},{9,10},{10,1... | collective-permute-start | bytes 331784 | tf_op jit(solution)/shard_map/ppermute | solution.py:21
  143.7 4.3 collective-permute-start.25
  144.6 5.2 %collective-permute-start.24 = (bf16[1,1,3,32,192]{4,2,3,1,0:T(4,128)(2,1)S(1)}, bf16[1,1,3,32,192]{4,2,3,1,0:T(4,128)(2,1)S(1)}, u32[]{:S(2)}, u32[]{:S(2)}) collective-permute-start(bf16[1,1,3,32,192]{4,2,3,1,0:T(4,128)(2,1)S(1)} %get-tuple-element.28), channel_id=1, source_target_pairs={{0,8},{8,16},{16,24},{24,0},{1,9},{9,17},{17,25},{25,1},{2,10},{10... | collective-permute-start | bytes 110600 | tf_op jit(solution)/shard_map/ppermute | solution.py:21
  150.0 5.6 %collective-permute-start.27 = (bf16[3,1,3,32,192]{4,2,3,1,0:T(4,128)(2,1)S(1)}, bf16[3,1,3,32,192]{4,2,3,1,0:T(4,128)(2,1)S(1)}, u32[]{:S(2)}, u32[]{:S(2)}) collective-permute-start(bf16[3,1,3,32,192]{4,2,3,1,0:T(4,128)(2,1)S(1)} %pad_maximum_fusion.21), channel_id=1, source_target_pairs={{1,0},{2,1},{3,2},{4,3},{5,4},{6,5},{7,6},{0,7},{9,8},{10,9},{11,1... | collective-permute-start | bytes 331784 | tf_op jit(solution)/shard_map/ppermute | solution.py:23
  150.5 7.3 %collective-permute-start.26 = (bf16[3,1,3,32,192]{4,2,3,1,0:T(4,128)(2,1)S(1)}, bf16[3,1,3,32,192]{4,2,3,1,0:T(4,128)(2,1)S(1)}, u32[]{:S(2)}, u32[]{:S(2)}) collective-permute-start(bf16[3,1,3,32,192]{4,2,3,1,0:T(4,128)(2,1)S(1)} %pad_maximum_fusion.21), channel_id=1, source_target_pairs={{0,1},{1,2},{2,3},{3,4},{4,5},{5,6},{6,7},{7,0},{8,9},{9,10},{10,1... | collective-permute-start | bytes 331784 | tf_op jit(solution)/shard_map/ppermute | solution.py:21
  168.6 5.2 %collective-permute-start.28 = (bf16[1,1,3,32,192]{4,2,3,1,0:T(4,128)(2,1)S(1)}, bf16[1,1,3,32,192]{4,2,3,1,0:T(4,128)(2,1)S(1)}, u32[]{:S(2)}, u32[]{:S(2)}) collective-permute-start(bf16[1,1,3,32,192]{4,2,3,1,0:T(4,128)(2,1)S(1)} %get-tuple-element.30), channel_id=1, source_target_pairs={{0,8},{8,16},{16,24},{24,0},{1,9},{9,17},{17,25},{25,1},{2,10},{10... | collective-permute-start | bytes 110600 | tf_op jit(solution)/shard_map/ppermute | solution.py:21
  173.9 5.2 %collective-permute-start.31 = (bf16[3,1,3,32,192]{4,2,3,1,0:T(4,128)(2,1)S(1)}, bf16[3,1,3,32,192]{4,2,3,1,0:T(4,128)(2,1)S(1)}, u32[]{:S(2)}, u32[]{:S(2)}) collective-permute-start(bf16[3,1,3,32,192]{4,2,3,1,0:T(4,128)(2,1)S(1)} %pad_maximum_fusion.22), channel_id=1, source_target_pairs={{1,0},{2,1},{3,2},{4,3},{5,4},{6,5},{7,6},{0,7},{9,8},{10,9},{11,1... | collective-permute-start | bytes 331784 | tf_op jit(solution)/shard_map/ppermute | solution.py:23
  174.2 6.9 %collective-permute-start.30 = (bf16[3,1,3,32,192]{4,2,3,1,0:T(4,128)(2,1)S(1)}, bf16[3,1,3,32,192]{4,2,3,1,0:T(4,128)(2,1)S(1)}, u32[]{:S(2)}, u32[]{:S(2)}) collective-permute-start(bf16[3,1,3,32,192]{4,2,3,1,0:T(4,128)(2,1)S(1)} %pad_maximum_fusion.22), channel_id=1, source_target_pairs={{0,1},{1,2},{2,3},{3,4},{4,5},{5,6},{6,7},{7,0},{8,9},{9,10},{10,1... | collective-permute-start | bytes 331784 | tf_op jit(solution)/shard_map/ppermute | solution.py:21
  236.4 4.8 %collective-permute-start.33 = (bf16[1,1,3,32,192]{4,3,2,1,0:T(8,128)(2,1)S(1)}, bf16[1,1,3,32,192]{4,3,2,1,0:T(8,128)(2,1)S(1)}, u32[]{:S(2)}, u32[]{:S(2)}) collective-permute-start(bf16[1,1,3,32,192]{4,3,2,1,0:T(8,128)(2,1)S(1)} %fusion.222), channel_id=1, source_target_pairs={{8,0},{16,8},{24,16},{0,24},{9,1},{17,9},{25,17},{1,25},{10,2},{18... | collective-permute-start | bytes 110600 | tf_op jit(solution)/shard_map/ppermute | solution.py:23
  238.8 5.0 %collective-permute-start.32 = (bf16[1,1,3,32,192]{4,3,2,1,0:T(8,128)(2,1)S(1)}, bf16[1,1,3,32,192]{4,3,2,1,0:T(8,128)(2,1)S(1)}, u32[]{:S(2)}, u32[]{:S(2)}) collective-permute-start(bf16[1,1,3,32,192]{4,3,2,1,0:T(8,128)(2,1)S(1)} %fusion.222), channel_id=1, source_target_pairs={{0,8},{8,16},{16,24},{24,0},{1,9},{9,17},{17,25},{25,1},{2,10},{10... | collective-permute-start | bytes 110600 | tf_op jit(solution)/shard_map/ppermute | solution.py:21
  243.9 6.5 %collective-permute-start.34 = (bf16[3,1,3,32,192]{4,3,2,1,0:T(8,128)(2,1)S(1)}, bf16[3,1,3,32,192]{4,3,2,1,0:T(8,128)(2,1)S(1)}, u32[]{:S(2)}, u32[]{:S(2)}) collective-permute-start(bf16[3,1,3,32,192]{4,3,2,1,0:T(8,128)(2,1)S(1)} %pad_maximum_fusion.24), channel_id=1, source_target_pairs={{0,1},{1,2},{2,3},{3,4},{4,5},{5,6},{6,7},{7,0},{8,9},{9,10},{10,1... | collective-permute-start | bytes 331784 | tf_op jit(solution)/shard_map/ppermute | solution.py:21
  260.2 5.0 %collective-permute-start.36 = (bf16[1,1,3,32,192]{4,3,2,1,0:T(8,128)(2,1)S(1)}, bf16[1,1,3,32,192]{4,3,2,1,0:T(8,128)(2,1)S(1)}, u32[]{:S(2)}, u32[]{:S(2)}) collective-permute-start(bf16[1,1,3,32,192]{4,3,2,1,0:T(8,128)(2,1)S(1)} %fusion.223), channel_id=1, source_target_pairs={{0,8},{8,16},{16,24},{24,0},{1,9},{9,17},{17,25},{25,1},{2,10},{10... | collective-permute-start | bytes 110600 | tf_op jit(solution)/shard_map/ppermute | solution.py:21
  265.3 6.4 %collective-permute-start.38 = (bf16[3,1,3,32,192]{4,3,2,1,0:T(8,128)(2,1)S(1)}, bf16[3,1,3,32,192]{4,3,2,1,0:T(8,128)(2,1)S(1)}, u32[]{:S(2)}, u32[]{:S(2)}) collective-permute-start(bf16[3,1,3,32,192]{4,3,2,1,0:T(8,128)(2,1)S(1)} %pad_maximum_fusion.25), channel_id=1, source_target_pairs={{0,1},{1,2},{2,3},{3,4},{4,5},{5,6},{6,7},{7,0},{8,9},{9,10},{10,1... | collective-permute-start | bytes 331784 | tf_op jit(solution)/shard_map/ppermute | solution.py:21
  282.4 5.0 %collective-permute-start.40 = (bf16[1,1,3,32,192]{4,3,2,1,0:T(8,128)(2,1)S(1)}, bf16[1,1,3,32,192]{4,3,2,1,0:T(8,128)(2,1)S(1)}, u32[]{:S(2)}, u32[]{:S(2)}) collective-permute-start(bf16[1,1,3,32,192]{4,3,2,1,0:T(8,128)(2,1)S(1)} %get-tuple-element.16), channel_id=1, source_target_pairs={{0,8},{8,16},{16,24},{24,0},{1,9},{9,17},{17,25},{25,1},{2,10},{10... | collective-permute-start | bytes 110600 | tf_op jit(solution)/shard_map/ppermute | solution.py:21
  287.6 6.6 %collective-permute-start.42 = (bf16[3,1,3,32,192]{4,3,2,1,0:T(8,128)(2,1)S(1)}, bf16[3,1,3,32,192]{4,3,2,1,0:T(8,128)(2,1)S(1)}, u32[]{:S(2)}, u32[]{:S(2)}) collective-permute-start(bf16[3,1,3,32,192]{4,3,2,1,0:T(8,128)(2,1)S(1)} %pad_maximum_fusion.26), channel_id=1, source_target_pairs={{0,1},{1,2},{2,3},{3,4},{4,5},{5,6},{6,7},{7,0},{8,9},{9,10},{10,1... | collective-permute-start | bytes 331784 | tf_op jit(solution)/shard_map/ppermute | solution.py:21
  304.0 5.0 %collective-permute-start.44 = (bf16[1,1,3,32,192]{4,3,2,1,0:T(8,128)(2,1)S(1)}, bf16[1,1,3,32,192]{4,3,2,1,0:T(8,128)(2,1)S(1)}, u32[]{:S(2)}, u32[]{:S(2)}) collective-permute-start(bf16[1,1,3,32,192]{4,3,2,1,0:T(8,128)(2,1)S(1)} %get-tuple-element.14), channel_id=1, source_target_pairs={{0,8},{8,16},{16,24},{24,0},{1,9},{9,17},{17,25},{25,1},{2,10},{10... | collective-permute-start | bytes 110600 | tf_op jit(solution)/shard_map/ppermute | solution.py:21
  309.1 6.4 %collective-permute-start.46 = (bf16[3,1,3,32,192]{4,3,2,1,0:T(8,128)(2,1)S(1)}, bf16[3,1,3,32,192]{4,3,2,1,0:T(8,128)(2,1)S(1)}, u32[]{:S(2)}, u32[]{:S(2)}) collective-permute-start(bf16[3,1,3,32,192]{4,3,2,1,0:T(8,128)(2,1)S(1)} %pad_maximum_fusion.27), channel_id=1, source_target_pairs={{0,1},{1,2},{2,3},{3,4},{4,5},{5,6},{6,7},{7,0},{8,9},{9,10},{10,1... | collective-permute-start | bytes 331784 | tf_op jit(solution)/shard_map/ppermute | solution.py:21
  325.3 5.0 %collective-permute-start.48 = (bf16[1,1,3,32,192]{4,3,2,1,0:T(8,128)(2,1)S(1)}, bf16[1,1,3,32,192]{4,3,2,1,0:T(8,128)(2,1)S(1)}, u32[]{:S(2)}, u32[]{:S(2)}) collective-permute-start(bf16[1,1,3,32,192]{4,3,2,1,0:T(8,128)(2,1)S(1)} %get-tuple-element.12), channel_id=1, source_target_pairs={{0,8},{8,16},{16,24},{24,0},{1,9},{9,17},{17,25},{25,1},{2,10},{10... | collective-permute-start | bytes 110600 | tf_op jit(solution)/shard_map/ppermute | solution.py:21
  330.4 6.8 %collective-permute-start.50 = (bf16[3,1,3,32,192]{4,3,2,1,0:T(8,128)(2,1)S(1)}, bf16[3,1,3,32,192]{4,3,2,1,0:T(8,128)(2,1)S(1)}, u32[]{:S(2)}, u32[]{:S(2)}) collective-permute-start(bf16[3,1,3,32,192]{4,3,2,1,0:T(8,128)(2,1)S(1)} %pad_maximum_fusion.28), channel_id=1, source_target_pairs={{0,1},{1,2},{2,3},{3,4},{4,5},{5,6},{6,7},{7,0},{8,9},{9,10},{10,1... | collective-permute-start | bytes 331784 | tf_op jit(solution)/shard_map/ppermute | solution.py:21
  347.5 5.0 %collective-permute-start.52 = (bf16[1,1,3,32,192]{4,3,2,1,0:T(8,128)(2,1)S(1)}, bf16[1,1,3,32,192]{4,3,2,1,0:T(8,128)(2,1)S(1)}, u32[]{:S(2)}, u32[]{:S(2)}) collective-permute-start(bf16[1,1,3,32,192]{4,3,2,1,0:T(8,128)(2,1)S(1)} %get-tuple-element.10), channel_id=1, source_target_pairs={{0,8},{8,16},{16,24},{24,0},{1,9},{9,17},{17,25},{25,1},{2,10},{10... | collective-permute-start | bytes 110600 | tf_op jit(solution)/shard_map/ppermute | solution.py:21
  352.6 6.4 %collective-permute-start.54 = (bf16[3,1,3,32,192]{4,3,2,1,0:T(8,128)(2,1)S(1)}, bf16[3,1,3,32,192]{4,3,2,1,0:T(8,128)(2,1)S(1)}, u32[]{:S(2)}, u32[]{:S(2)}) collective-permute-start(bf16[3,1,3,32,192]{4,3,2,1,0:T(8,128)(2,1)S(1)} %pad_maximum_fusion.29), channel_id=1, source_target_pairs={{0,1},{1,2},{2,3},{3,4},{4,5},{5,6},{6,7},{7,0},{8,9},{9,10},{10,1... | collective-permute-start | bytes 331784 | tf_op jit(solution)/shard_map/ppermute | solution.py:21
  369.2 5.0 %collective-permute-start.56 = (bf16[1,1,3,32,192]{4,3,2,1,0:T(8,128)(2,1)S(1)}, bf16[1,1,3,32,192]{4,3,2,1,0:T(8,128)(2,1)S(1)}, u32[]{:S(2)}, u32[]{:S(2)}) collective-permute-start(bf16[1,1,3,32,192]{4,3,2,1,0:T(8,128)(2,1)S(1)} %get-tuple-element.6), channel_id=1, source_target_pairs={{0,8},{8,16},{16,24},{24,0},{1,9},{9,17},{17,25},{25,1},{2,10},{10... | collective-permute-start | bytes 110600 | tf_op jit(solution)/shard_map/ppermute | solution.py:21
  374.3 6.6 %collective-permute-start.58 = (bf16[3,1,3,32,192]{4,3,2,1,0:T(8,128)(2,1)S(1)}, bf16[3,1,3,32,192]{4,3,2,1,0:T(8,128)(2,1)S(1)}, u32[]{:S(2)}, u32[]{:S(2)}) collective-permute-start(bf16[3,1,3,32,192]{4,3,2,1,0:T(8,128)(2,1)S(1)} %pad_maximum_fusion.30), channel_id=1, source_target_pairs={{0,1},{1,2},{2,3},{3,4},{4,5},{5,6},{6,7},{7,0},{8,9},{9,10},{10,1... | collective-permute-start | bytes 331784 | tf_op jit(solution)/shard_map/ppermute | solution.py:21
  390.7 5.0 %collective-permute-start.60 = (bf16[1,1,3,32,192]{4,3,2,1,0:T(8,128)(2,1)S(1)}, bf16[1,1,3,32,192]{4,3,2,1,0:T(8,128)(2,1)S(1)}, u32[]{:S(2)}, u32[]{:S(2)}) collective-permute-start(bf16[1,1,3,32,192]{4,3,2,1,0:T(8,128)(2,1)S(1)} %convert_bitcast_fusion), channel_id=1, source_target_pairs={{0,8},{8,16},{16,24},{24,0},{1,9},{9,17},{17,25},{25,1},{2,10},{10... | collective-permute-start | bytes 110600 | tf_op jit(solution)/shard_map/ppermute | solution.py:21
  395.8 6.4 %collective-permute-start.62 = (bf16[3,1,3,32,192]{4,3,2,1,0:T(8,128)(2,1)S(1)}, bf16[3,1,3,32,192]{4,3,2,1,0:T(8,128)(2,1)S(1)}, u32[]{:S(2)}, u32[]{:S(2)}) collective-permute-start(bf16[3,1,3,32,192]{4,3,2,1,0:T(8,128)(2,1)S(1)} %pad_maximum_fusion.31), channel_id=1, source_target_pairs={{0,1},{1,2},{2,3},{3,4},{4,5},{5,6},{6,7},{7,0},{8,9},{9,10},{10,1... | collective-permute-start | bytes 331784 | tf_op jit(solution)/shard_map/ppermute | solution.py:21
  (18 other events, 77.3 us)
where the time goes:
time: 466 us; the launch traced here: 457 us
  waiting for transfers between devices  164 us (35%)
  matrix products  136 us (29%)
  blocking collectives  75.9 us (16%)
  starting transfers between devices  47.7 us (10%)
  other arithmetic  22.3 us (5%)
  local copies, waits for them, and re-layouts  11.6 us (2%)
    ppermute x32, waiting for transfers between devices, with_halo(): lax.ppermute(head, axis, [((i + 1) % count, i) for i in range(count)])  95.2 us
    dot_general x16, matrix products, apply_operator(): jnp.einsum('kvj,kij->kvi', picked, matrices, preferred_element_type=jnp.f...  92.9 us
    psum x2, blocking collectives, orthonormal(): gram_matrix = lax.psum(partial_gram, ('gx', 'gy'))  75.9 us
    ppermute x32, waiting for transfers between devices, with_halo(): lax.ppermute(tail, axis, [(i, (i + 1) % count) for i in range(count)])  68.3 us
    dot_general x16, matrix products, apply_operator(): jnp.einsum('zk,kvi->zvi', select, products, precision=lax.Precision.HIGHEST)  40.6 us
    ppermute x32, starting transfers between devices, with_halo(): lax.ppermute(tail, axis, [(i, (i + 1) % count) for i in range(count)])  24.6 us
    ppermute x32, starting transfers between devices, with_halo(): lax.ppermute(head, axis, [((i + 1) % count, i) for i in range(count)])  23.1 us
    gather x16, local copies, waits for them, and re-layouts, apply_operator(): picked = jnp.take(window_cells, sources, axis=0)  10.9 us
  transfers between devices with their start and end apart: 64, of which 64 were waited for; matrix products, arithmetic and copies ran while one was open for 0% of the time, Pallas kernels for 0%

commit v1 on v0

--- a/solution.py
+++ b/solution.py
@@ -32,7 +32,7 @@
     partial_gram = jnp.einsum(
         "zvd,zwd->vw", local_block, local_block, precision=lax.Precision.HIGHEST
     )
-    gram_matrix = lax.psum(partial_gram, ("gx", "gy"))
+    gram_matrix = jax.lax.psum(jax.lax.psum(partial_gram, "gy"), "gx")
     factor = jnp.linalg.cholesky(gram_matrix)
     identity = jnp.eye(local_block.shape[1], dtype=jnp.float32)
     inverse = jax.scipy.linalg.solve_triangular(factor, identity, lower=True)

time: 466 us -> 472 us (1.013)
  blocking collectives: 75.9 us -> 84 us
    psum x2 -> x4, blocking collectives: 75.9 us -> 84 us  [orthonormal(): gram_matrix = jax.lax.psum(jax.lax.psum(partial_gram, 'gy'), 'gx')]
where the time goes in v1:
time: 472 us; the launch traced here: 464 us
  waiting for transfers between devices  162 us (34%)
  matrix products  136 us (29%)
  blocking collectives  84 us (18%)
  starting transfers between devices  47.4 us (10%)
  other arithmetic  22.3 us (5%)
  local copies, waits for them, and re-layouts  11.6 us (2%)
    ppermute x32, waiting for transfers between devices, with_halo(): lax.ppermute(head, axis, [((i + 1) % count, i) for i in range(count)])  95.9 us
    dot_general x16, matrix products, apply_operator(): jnp.einsum('kvj,kij->kvi', picked, matrices, preferred_element_type=jnp.f...  92.9 us
    psum x4, blocking collectives, orthonormal(): gram_matrix = jax.lax.psum(jax.lax.psum(partial_gram, 'gy'), 'gx')  84 us
    ppermute x32, waiting for transfers between devices, with_halo(): lax.ppermute(tail, axis, [(i, (i + 1) % count) for i in range(count)])  66.2 us
    dot_general x16, matrix products, apply_operator(): jnp.einsum('zk,kvi->zvi', select, products, precision=lax.Precision.HIGHEST)  40.6 us
    ppermute x32, starting transfers between devices, with_halo(): lax.ppermute(tail, axis, [(i, (i + 1) % count) for i in range(count)])  25.9 us
    ppermute x32, starting transfers between devices, with_halo(): lax.ppermute(head, axis, [((i + 1) % count, i) for i in range(count)])  21.5 us
    gather x16, local copies, waits for them, and re-layouts, apply_operator(): picked = jnp.take(window_cells, sources, axis=0)  10.9 us
  transfers between devices with their start and end apart: 64, of which 64 were waited for; matrix products, arithmetic and copies ran while one was open for 0% of the time, Pallas kernels for 0%

profile of v1, /device:TPU:0, one launch (start us, length us, event | category | flops | bytes accessed | tf_op | source)
XLA Modules:
  0.0 463.7 jit_solution(6448188568971137154)
XLA Ops:
  0.9 3.9 collective-permute-start.1
  6.5 3.2 collective-permute-done
  11.5 3.7 collective-permute-done.3
  15.2 3.0 collective-permute-done.2
  19.0 5.8 %fusion.30 = f32[81,32,192]{2,1,0:T(8,128)S(1)} fusion(bf16[1,1,81,192,192]{4,3,2,1,0:T(8,128)(2,1)} %param.10, bf16[81,32,192]{2,1,0:T(8,128)(2,1)S(1)} %gather_fusion, pred[81]{0:T(512)(128)(4,1)S(1)} %compare_and_fusion), kind=kOutput, calls=%fused_computation.46 | convolution fusion | flops 191600640 | bytes 8958033 | tf_op jit(solution)/shard_map/kvj,kij->kvi/dot_general | solution.py:60
  24.9 2.6 multiply_convert_fusion
  33.4 4.6 collective-permute-done.7
  41.6 5.8 %fusion.28 = f32[81,32,192]{2,1,0:T(8,128)S(1)} fusion(bf16[1,1,81,192,192]{4,3,2,1,0:T(8,128)(2,1)} %param.10, bf16[81,32,192]{2,1,0:T(8,128)(2,1)S(1)} %gather_fusion.1, pred[81]{0:T(512)(128)(4,1)S(1)} %compare_and_fusion), kind=kOutput, calls=%fused_computation.44 | convolution fusion | flops 191600640 | bytes 8958033 | tf_op jit(solution)/shard_map/kvj,kij->kvi/dot_general | solution.py:60
  47.4 2.6 fusion.269
  57.8 3.8 collective-permute-done.11
  61.6 3.1 collective-permute-done.10
  66.1 5.8 %fusion.26 = f32[81,32,192]{2,1,0:T(8,128)S(1)} fusion(bf16[1,1,81,192,192]{4,3,2,1,0:T(8,128)(2,1)} %param.10, bf16[81,32,192]{2,1,0:T(8,128)(2,1)S(1)} %gather_fusion.2, pred[81]{0:T(512)(128)(4,1)S(1)} %compare_and_fusion), kind=kOutput, calls=%fused_computation.42 | convolution fusion | flops 191600640 | bytes 8958033 | tf_op jit(solution)/shard_map/kvj,kij->kvi/dot_general | solution.py:60
  71.9 2.5 fusion.270
  81.3 4.6 collective-permute-done.15
  89.1 5.8 %fusion.24 = f32[81,32,192]{2,1,0:T(8,128)S(1)} fusion(bf16[1,1,81,192,192]{4,3,2,1,0:T(8,128)(2,1)} %param.10, bf16[81,32,192]{2,1,0:T(8,128)(2,1)S(1)} %gather_fusion.3, pred[81]{0:T(512)(128)(4,1)S(1)} %compare_and_fusion), kind=kOutput, calls=%fused_computation.40 | convolution fusion | flops 191600640 | bytes 8958033 | tf_op jit(solution)/shard_map/kvj,kij->kvi/dot_general | solution.py:60
  94.9 2.5 fusion.271
  104.5 4.8 %collective-permute-done.19 = bf16[3,1,3,32,192]{4,2,3,1,0:T(4,128)(2,1)S(1)} collective-permute-done((bf16[3,1,3,32,192]{4,2,3,1,0:T(4,128)(2,1)S(1)}, bf16[3,1,3,32,192]{4,2,3,1,0:T(4,128)(2,1)S(1)}, u32[]{:S(2)}, u32[]{:S(2)}) %collective-permute-start.19) | collective-permute-done | bytes 110624 | tf_op jit(solution)/shard_map/ppermute | solution.py:23
  112.7 5.8 %fusion.22 = f32[81,32,192]{2,1,0:T(8,128)S(1)} fusion(bf16[1,1,81,192,192]{4,3,2,1,0:T(8,128)(2,1)} %param.10, bf16[81,32,192]{2,1,0:T(8,128)(2,1)S(1)} %gather_fusion.4, pred[81]{0:T(512)(128)(4,1)S(1)} %compare_and_fusion), kind=kOutput, calls=%fused_computation.38 | convolution fusion | flops 191600640 | bytes 8958033 | tf_op jit(solution)/shard_map/kvj,kij->kvi/dot_general | solution.py:60
  127.5 4.6 collective-permute-done.23
  135.3 5.8 %fusion.20 = f32[81,32,192]{2,1,0:T(8,128)S(1)} fusion(bf16[1,1,81,192,192]{4,3,2,1,0:T(8,128)(2,1)} %param.10, bf16[81,32,192]{2,1,0:T(8,128)(2,1)S(1)} %gather_fusion.5, pred[81]{0:T(512)(128)(4,1)S(1)} %compare_and_fusion), kind=kOutput, calls=%fused_computation.36 | convolution fusion | flops 191600640 | bytes 8958033 | tf_op jit(solution)/shard_map/kvj,kij->kvi/dot_general | solution.py:60
  150.9 4.6 collective-permute-done.27
  159.1 5.8 %fusion.18 = f32[81,32,192]{2,1,0:T(8,128)S(1)} fusion(bf16[1,1,81,192,192]{4,3,2,1,0:T(8,128)(2,1)} %param.10, bf16[81,32,192]{2,1,0:T(8,128)(2,1)S(1)} %gather_fusion.6, pred[81]{0:T(512)(128)(4,1)S(1)} %compare_and_fusion), kind=kOutput, calls=%fused_computation.34 | convolution fusion | flops 191600640 | bytes 8958033 | tf_op jit(solution)/shard_map/kvj,kij->kvi/dot_general | solution.py:60
  164.9 2.5 fusion.274
  174.5 4.6 collective-permute-done.31
  182.4 5.8 %fusion.16 = f32[81,32,192]{2,1,0:T(8,128)S(1)} fusion(bf16[1,1,81,192,192]{4,3,2,1,0:T(8,128)(2,1)} %param.10, bf16[81,32,192]{2,1,0:T(8,128)(2,1)S(1)} %gather_fusion.7, pred[81]{0:T(512)(128)(4,1)S(1)} %compare_and_fusion), kind=kOutput, calls=%fused_computation.32 | convolution fusion | flops 191600640 | bytes 8958033 | tf_op jit(solution)/shard_map/kvj,kij->kvi/dot_general | solution.py:60
  191.0 27.5 %psum.28 = f32[32,32]{0,1:T(8,128)S(1)} all-reduce(f32[32,32]{0,1:T(8,128)S(1)} %convolution_bitcast_fusion.3), channel_id=1, replica_groups=mesh['gx'=4,'gy'=8] {'gy'}, use_global_device_ids=true, to_apply=%region_0.0 | all-reduce | flops 1024 | bytes 8192 | tf_op jit(solution)/shard_map/psum | solution.py:35
  218.5 14.4 %psum.29 = f32[32,32]{0,1:T(8,128)S(1)} all-reduce(f32[32,32]{0,1:T(8,128)S(1)} %psum.28), channel_id=1, replica_groups=mesh['gx'=4,'gy'=8] {'gx'}, use_global_device_ids=true, to_apply=%region_1.3 | all-reduce | flops 1024 | bytes 8192 | tf_op jit(solution)/shard_map/psum | solution.py:35
  233.0 2.9 cholesky.44
  247.2 3.6 collective-permute-done.35
  253.9 5.8 %fusion.14 = f32[81,32,192]{2,1,0:T(8,128)S(1)} fusion(bf16[1,1,81,192,192]{4,3,2,1,0:T(8,128)(2,1)} %param.10, bf16[81,32,192]{2,1,0:T(8,128)(2,1)S(1)} %gather_fusion.8, pred[81]{0:T(512)(128)(4,1)S(1)} %compare_and_fusion), kind=kOutput, calls=%fused_computation.30 | convolution fusion | flops 191600640 | bytes 8958033 | tf_op jit(solution)/shard_map/kvj,kij->kvi/dot_general | solution.py:60
  268.1 3.6 collective-permute-done.39
  274.8 5.8 %fusion.12 = f32[81,32,192]{2,1,0:T(8,128)S(1)} fusion(bf16[1,1,81,192,192]{4,3,2,1,0:T(8,128)(2,1)} %param.10, bf16[81,32,192]{2,1,0:T(8,128)(2,1)S(1)} %gather_fusion.9, pred[81]{0:T(512)(128)(4,1)S(1)} %compare_and_fusion), kind=kOutput, calls=%fused_computation.28 | convolution fusion | flops 191600640 | bytes 8958033 | tf_op jit(solution)/shard_map/kvj,kij->kvi/dot_general | solution.py:60
  290.2 3.5 collective-permute-done.43
  296.9 5.8 %fusion.10 = f32[81,32,192]{2,1,0:T(8,128)S(1)} fusion(bf16[1,1,81,192,192]{4,3,2,1,0:T(8,128)(2,1)} %param.10, bf16[81,32,192]{2,1,0:T(8,128)(2,1)S(1)} %gather_fusion.10, pred[81]{0:T(512)(128)(4,1)S(1)} %compare_and_fusion), kind=kOutput, calls=%fused_computation.26 | convolution fusion | flops 191600640 | bytes 8958033 | tf_op jit(solution)/shard_map/kvj,kij->kvi/dot_general | solution.py:60
  311.5 3.6 collective-permute-done.47
  318.2 5.8 %fusion.8 = f32[81,32,192]{2,1,0:T(8,128)S(1)} fusion(bf16[1,1,81,192,192]{4,3,2,1,0:T(8,128)(2,1)} %param.10, bf16[81,32,192]{2,1,0:T(8,128)(2,1)S(1)} %gather_fusion.11, pred[81]{0:T(512)(128)(4,1)S(1)} %compare_and_fusion), kind=kOutput, calls=%fused_computation.24 | convolution fusion | flops 191600640 | bytes 8958033 | tf_op jit(solution)/shard_map/kvj,kij->kvi/dot_general | solution.py:60
  334.1 3.1 collective-permute-done.51
  337.2 2.8 collective-permute-done.50
  340.8 5.8 %fusion.6 = f32[81,32,192]{2,1,0:T(8,128)S(1)} fusion(bf16[1,1,81,192,192]{4,3,2,1,0:T(8,128)(2,1)} %param.10, bf16[81,32,192]{2,1,0:T(8,128)(2,1)S(1)} %gather_fusion.12, pred[81]{0:T(512)(128)(4,1)S(1)} %compare_and_fusion), kind=kOutput, calls=%fused_computation.22 | convolution fusion | flops 191600640 | bytes 8958033 | tf_op jit(solution)/shard_map/kvj,kij->kvi/dot_general | solution.py:60
  355.0 3.6 collective-permute-done.55
  361.7 5.8 %fusion.4 = f32[81,32,192]{2,1,0:T(8,128)S(1)} fusion(bf16[1,1,81,192,192]{4,3,2,1,0:T(8,128)(2,1)} %param.10, bf16[81,32,192]{2,1,0:T(8,128)(2,1)S(1)} %gather_fusion.13, pred[81]{0:T(512)(128)(4,1)S(1)} %compare_and_fusion), kind=kOutput, calls=%fused_computation.20 | convolution fusion | flops 191600640 | bytes 8958033 | tf_op jit(solution)/shard_map/kvj,kij->kvi/dot_general | solution.py:60
  376.9 3.6 collective-permute-done.59
  383.6 5.8 %fusion.2 = f32[81,32,192]{2,1,0:T(8,128)S(1)} fusion(bf16[1,1,81,192,192]{4,3,2,1,0:T(8,128)(2,1)} %param.10, bf16[81,32,192]{2,1,0:T(8,128)(2,1)S(1)} %gather_fusion.14, pred[81]{0:T(512)(128)(4,1)S(1)} %compare_and_fusion), kind=kOutput, calls=%fused_computation.18 | convolution fusion | flops 191600640 | bytes 8958033 | tf_op jit(solution)/shard_map/kvj,kij->kvi/dot_general | solution.py:60
  398.2 3.6 collective-permute-done.63
  404.9 5.8 %fusion = f32[81,32,192]{2,1,0:T(8,128)S(1)} fusion(bf16[1,1,81,192,192]{4,3,2,1,0:T(8,128)(2,1)} %param.10, bf16[81,32,192]{2,1,0:T(8,128)(2,1)S(1)} %gather_fusion.15, pred[81]{0:T(512)(128)(4,1)S(1)} %compare_and_fusion), kind=kOutput, calls=%fused_computation.16 | convolution fusion | flops 191600640 | bytes 8958033 | tf_op jit(solution)/shard_map/kvj,kij->kvi/dot_general | solution.py:60
  413.6 27.1 %psum.30 = f32[32,32]{0,1:T(8,128)S(1)} all-reduce(f32[32,32]{0,1:T(8,128)S(1)} %convolution_bitcast_fusion.1), channel_id=1, replica_groups=mesh['gx'=4,'gy'=8] {'gy'}, use_global_device_ids=true, to_apply=%region_4.8 | all-reduce | flops 1024 | bytes 8192 | tf_op jit(solution)/shard_map/psum | solution.py:35
  440.7 15.0 %psum.31 = f32[32,32]{0,1:T(8,128)S(1)} all-reduce(f32[32,32]{0,1:T(8,128)S(1)} %psum.30), channel_id=1, replica_groups=mesh['gx'=4,'gy'=8] {'gx'}, use_global_device_ids=true, to_apply=%region_5.9 | all-reduce | flops 1024 | bytes 8192 | tf_op jit(solution)/shard_map/psum | solution.py:35
  455.7 2.9 cholesky.55
  (208 shorter events, 188.1 us)
Async XLA Ops:
  0.9 5.6 %collective-permute-start.1 = (bf16[1,1,3,32,192]{4,3,2,1,0:T(8,128)(2,1)S(1)}, bf16[1,1,3,32,192]{4,3,2,1,0:T(8,128)(2,1)S(1)}, u32[]{:S(2)}, u32[]{:S(2)}) collective-permute-start(bf16[1,1,3,32,192]{4,3,2,1,0:T(8,128)(2,1)S(1)} %convert_element_type.82), channel_id=1, source_target_pairs={{8,0},{16,8},{24,16},{0,24},{9,1},{17,9},{25,17},{1,25},{10,2},{18... | collective-permute-start | bytes 110600 | tf_op jit(solution)/shard_map/ppermute | solution.py:23
  4.8 5.0 %collective-permute-start = (bf16[1,1,3,32,192]{4,3,2,1,0:T(8,128)(2,1)S(1)}, bf16[1,1,3,32,192]{4,3,2,1,0:T(8,128)(2,1)S(1)}, u32[]{:S(2)}, u32[]{:S(2)}) collective-permute-start(bf16[1,1,3,32,192]{4,3,2,1,0:T(8,128)(2,1)S(1)} %convert_element_type.82), channel_id=1, source_target_pairs={{0,8},{8,16},{16,24},{24,0},{1,9},{9,17},{17,25},{25,1},{2,10},{10... | collective-permute-start | bytes 110600 | tf_op jit(solution)/shard_map/ppermute | solution.py:21
  9.8 5.4 %collective-permute-start.3 = (bf16[3,1,3,32,192]{4,3,2,1,0:T(8,128)(2,1)S(1)}, bf16[3,1,3,32,192]{4,3,2,1,0:T(8,128)(2,1)S(1)}, u32[]{:S(2)}, u32[]{:S(2)}) collective-permute-start(bf16[3,1,3,32,192]{4,3,2,1,0:T(8,128)(2,1)S(1)} %pad_maximum_fusion.23), channel_id=1, source_target_pairs={{1,0},{2,1},{3,2},{4,3},{5,4},{6,5},{7,6},{0,7},{9,8},{10,9},{11,1... | collective-permute-start | bytes 331784 | tf_op jit(solution)/shard_map/ppermute | solution.py:23
  11.5 6.7 %collective-permute-start.2 = (bf16[3,1,3,32,192]{4,3,2,1,0:T(8,128)(2,1)S(1)}, bf16[3,1,3,32,192]{4,3,2,1,0:T(8,128)(2,1)S(1)}, u32[]{:S(2)}, u32[]{:S(2)}) collective-permute-start(bf16[3,1,3,32,192]{4,3,2,1,0:T(8,128)(2,1)S(1)} %pad_maximum_fusion.23), channel_id=1, source_target_pairs={{0,1},{1,2},{2,3},{3,4},{4,5},{5,6},{6,7},{7,0},{8,9},{9,10},{10,1... | collective-permute-start | bytes 331784 | tf_op jit(solution)/shard_map/ppermute | solution.py:21
  27.4 4.3 collective-permute-start.5
  27.5 5.2 %collective-permute-start.4 = (bf16[1,1,3,32,192]{4,2,3,1,0:T(4,128)(2,1)S(1)}, bf16[1,1,3,32,192]{4,2,3,1,0:T(4,128)(2,1)S(1)}, u32[]{:S(2)}, u32[]{:S(2)}) collective-permute-start(bf16[1,1,3,32,192]{4,2,3,1,0:T(4,128)(2,1)S(1)} %get-tuple-element.18), channel_id=1, source_target_pairs={{0,8},{8,16},{16,24},{24,0},{1,9},{9,17},{17,25},{25,1},{2,10},{10... | collective-permute-start | bytes 110600 | tf_op jit(solution)/shard_map/ppermute | solution.py:21
  32.9 5.2 %collective-permute-start.7 = (bf16[3,1,3,32,192]{4,2,3,1,0:T(4,128)(2,1)S(1)}, bf16[3,1,3,32,192]{4,2,3,1,0:T(4,128)(2,1)S(1)}, u32[]{:S(2)}, u32[]{:S(2)}) collective-permute-start(bf16[3,1,3,32,192]{4,2,3,1,0:T(4,128)(2,1)S(1)} %pad_maximum_fusion.16), channel_id=1, source_target_pairs={{1,0},{2,1},{3,2},{4,3},{5,4},{6,5},{7,6},{0,7},{9,8},{10,9},{11,1... | collective-permute-start | bytes 331784 | tf_op jit(solution)/shard_map/ppermute | solution.py:23
  32.9 7.3 %collective-permute-start.6 = (bf16[3,1,3,32,192]{4,2,3,1,0:T(4,128)(2,1)S(1)}, bf16[3,1,3,32,192]{4,2,3,1,0:T(4,128)(2,1)S(1)}, u32[]{:S(2)}, u32[]{:S(2)}) collective-permute-start(bf16[3,1,3,32,192]{4,2,3,1,0:T(4,128)(2,1)S(1)} %pad_maximum_fusion.16), channel_id=1, source_target_pairs={{0,1},{1,2},{2,3},{3,4},{4,5},{5,6},{6,7},{7,0},{8,9},{9,10},{10,1... | collective-permute-start | bytes 331784 | tf_op jit(solution)/shard_map/ppermute | solution.py:21
  50.0 4.3 collective-permute-start.9
  50.9 5.2 %collective-permute-start.8 = (bf16[1,1,3,32,192]{4,2,3,1,0:T(4,128)(2,1)S(1)}, bf16[1,1,3,32,192]{4,2,3,1,0:T(4,128)(2,1)S(1)}, u32[]{:S(2)}, u32[]{:S(2)}) collective-permute-start(bf16[1,1,3,32,192]{4,2,3,1,0:T(4,128)(2,1)S(1)} %get-tuple-element.20), channel_id=1, source_target_pairs={{0,8},{8,16},{16,24},{24,0},{1,9},{9,17},{17,25},{25,1},{2,10},{10... | collective-permute-start | bytes 110600 | tf_op jit(solution)/shard_map/ppermute | solution.py:21
  56.3 5.3 %collective-permute-start.11 = (bf16[3,1,3,32,192]{4,2,3,1,0:T(4,128)(2,1)S(1)}, bf16[3,1,3,32,192]{4,2,3,1,0:T(4,128)(2,1)S(1)}, u32[]{:S(2)}, u32[]{:S(2)}) collective-permute-start(bf16[3,1,3,32,192]{4,2,3,1,0:T(4,128)(2,1)S(1)} %pad_maximum_fusion.17), channel_id=1, source_target_pairs={{1,0},{2,1},{3,2},{4,3},{5,4},{6,5},{7,6},{0,7},{9,8},{10,9},{11,1... | collective-permute-start | bytes 331784 | tf_op jit(solution)/shard_map/ppermute | solution.py:23
  57.7 7.0 %collective-permute-start.10 = (bf16[3,1,3,32,192]{4,2,3,1,0:T(4,128)(2,1)S(1)}, bf16[3,1,3,32,192]{4,2,3,1,0:T(4,128)(2,1)S(1)}, u32[]{:S(2)}, u32[]{:S(2)}) collective-permute-start(bf16[3,1,3,32,192]{4,2,3,1,0:T(4,128)(2,1)S(1)} %pad_maximum_fusion.17), channel_id=1, source_target_pairs={{0,1},{1,2},{2,3},{3,4},{4,5},{5,6},{6,7},{7,0},{8,9},{9,10},{10,1... | collective-permute-start | bytes 331784 | tf_op jit(solution)/shard_map/ppermute | solution.py:21
  74.4 4.3 collective-permute-start.13
  75.4 5.2 %collective-permute-start.12 = (bf16[1,1,3,32,192]{4,2,3,1,0:T(4,128)(2,1)S(1)}, bf16[1,1,3,32,192]{4,2,3,1,0:T(4,128)(2,1)S(1)}, u32[]{:S(2)}, u32[]{:S(2)}) collective-permute-start(bf16[1,1,3,32,192]{4,2,3,1,0:T(4,128)(2,1)S(1)} %get-tuple-element.22), channel_id=1, source_target_pairs={{0,8},{8,16},{16,24},{24,0},{1,9},{9,17},{17,25},{25,1},{2,10},{10... | collective-permute-start | bytes 110600 | tf_op jit(solution)/shard_map/ppermute | solution.py:21
  80.8 5.2 %collective-permute-start.15 = (bf16[3,1,3,32,192]{4,2,3,1,0:T(4,128)(2,1)S(1)}, bf16[3,1,3,32,192]{4,2,3,1,0:T(4,128)(2,1)S(1)}, u32[]{:S(2)}, u32[]{:S(2)}) collective-permute-start(bf16[3,1,3,32,192]{4,2,3,1,0:T(4,128)(2,1)S(1)} %pad_maximum_fusion.18), channel_id=1, source_target_pairs={{1,0},{2,1},{3,2},{4,3},{5,4},{6,5},{7,6},{0,7},{9,8},{10,9},{11,1... | collective-permute-start | bytes 331784 | tf_op jit(solution)/shard_map/ppermute | solution.py:23
  80.8 6.9 %collective-permute-start.14 = (bf16[3,1,3,32,192]{4,2,3,1,0:T(4,128)(2,1)S(1)}, bf16[3,1,3,32,192]{4,2,3,1,0:T(4,128)(2,1)S(1)}, u32[]{:S(2)}, u32[]{:S(2)}) collective-permute-start(bf16[3,1,3,32,192]{4,2,3,1,0:T(4,128)(2,1)S(1)} %pad_maximum_fusion.18), channel_id=1, source_target_pairs={{0,1},{1,2},{2,3},{3,4},{4,5},{5,6},{6,7},{7,0},{8,9},{9,10},{10,1... | collective-permute-start | bytes 331784 | tf_op jit(solution)/shard_map/ppermute | solution.py:21
  97.5 4.3 collective-permute-start.17
  98.4 5.2 %collective-permute-start.16 = (bf16[1,1,3,32,192]{4,2,3,1,0:T(4,128)(2,1)S(1)}, bf16[1,1,3,32,192]{4,2,3,1,0:T(4,128)(2,1)S(1)}, u32[]{:S(2)}, u32[]{:S(2)}) collective-permute-start(bf16[1,1,3,32,192]{4,2,3,1,0:T(4,128)(2,1)S(1)} %get-tuple-element.24), channel_id=1, source_target_pairs={{0,8},{8,16},{16,24},{24,0},{1,9},{9,17},{17,25},{25,1},{2,10},{10... | collective-permute-start | bytes 110600 | tf_op jit(solution)/shard_map/ppermute | solution.py:21
  103.8 5.5 %collective-permute-start.19 = (bf16[3,1,3,32,192]{4,2,3,1,0:T(4,128)(2,1)S(1)}, bf16[3,1,3,32,192]{4,2,3,1,0:T(4,128)(2,1)S(1)}, u32[]{:S(2)}, u32[]{:S(2)}) collective-permute-start(bf16[3,1,3,32,192]{4,2,3,1,0:T(4,128)(2,1)S(1)} %pad_maximum_fusion.19), channel_id=1, source_target_pairs={{1,0},{2,1},{3,2},{4,3},{5,4},{6,5},{7,6},{0,7},{9,8},{10,9},{11,1... | collective-permute-start | bytes 331784 | tf_op jit(solution)/shard_map/ppermute | solution.py:23
  104.2 7.1 %collective-permute-start.18 = (bf16[3,1,3,32,192]{4,2,3,1,0:T(4,128)(2,1)S(1)}, bf16[3,1,3,32,192]{4,2,3,1,0:T(4,128)(2,1)S(1)}, u32[]{:S(2)}, u32[]{:S(2)}) collective-permute-start(bf16[3,1,3,32,192]{4,2,3,1,0:T(4,128)(2,1)S(1)} %pad_maximum_fusion.19), channel_id=1, source_target_pairs={{0,1},{1,2},{2,3},{3,4},{4,5},{5,6},{6,7},{7,0},{8,9},{9,10},{10,1... | collective-permute-start | bytes 331784 | tf_op jit(solution)/shard_map/ppermute | solution.py:21
  121.0 4.3 collective-permute-start.21
  121.6 5.2 %collective-permute-start.20 = (bf16[1,1,3,32,192]{4,2,3,1,0:T(4,128)(2,1)S(1)}, bf16[1,1,3,32,192]{4,2,3,1,0:T(4,128)(2,1)S(1)}, u32[]{:S(2)}, u32[]{:S(2)}) collective-permute-start(bf16[1,1,3,32,192]{4,2,3,1,0:T(4,128)(2,1)S(1)} %get-tuple-element.26), channel_id=1, source_target_pairs={{0,8},{8,16},{16,24},{24,0},{1,9},{9,17},{17,25},{25,1},{2,10},{10... | collective-permute-start | bytes 110600 | tf_op jit(solution)/shard_map/ppermute | solution.py:21
  127.0 5.2 %collective-permute-start.23 = (bf16[3,1,3,32,192]{4,2,3,1,0:T(4,128)(2,1)S(1)}, bf16[3,1,3,32,192]{4,2,3,1,0:T(4,128)(2,1)S(1)}, u32[]{:S(2)}, u32[]{:S(2)}) collective-permute-start(bf16[3,1,3,32,192]{4,2,3,1,0:T(4,128)(2,1)S(1)} %pad_maximum_fusion.20), channel_id=1, source_target_pairs={{1,0},{2,1},{3,2},{4,3},{5,4},{6,5},{7,6},{0,7},{9,8},{10,9},{11,1... | collective-permute-start | bytes 331784 | tf_op jit(solution)/shard_map/ppermute | solution.py:23
  127.0 6.9 %collective-permute-start.22 = (bf16[3,1,3,32,192]{4,2,3,1,0:T(4,128)(2,1)S(1)}, bf16[3,1,3,32,192]{4,2,3,1,0:T(4,128)(2,1)S(1)}, u32[]{:S(2)}, u32[]{:S(2)}) collective-permute-start(bf16[3,1,3,32,192]{4,2,3,1,0:T(4,128)(2,1)S(1)} %pad_maximum_fusion.20), channel_id=1, source_target_pairs={{0,1},{1,2},{2,3},{3,4},{4,5},{5,6},{6,7},{7,0},{8,9},{9,10},{10,1... | collective-permute-start | bytes 331784 | tf_op jit(solution)/shard_map/ppermute | solution.py:21
  143.7 4.3 collective-permute-start.25
  144.6 5.2 %collective-permute-start.24 = (bf16[1,1,3,32,192]{4,2,3,1,0:T(4,128)(2,1)S(1)}, bf16[1,1,3,32,192]{4,2,3,1,0:T(4,128)(2,1)S(1)}, u32[]{:S(2)}, u32[]{:S(2)}) collective-permute-start(bf16[1,1,3,32,192]{4,2,3,1,0:T(4,128)(2,1)S(1)} %get-tuple-element.28), channel_id=1, source_target_pairs={{0,8},{8,16},{16,24},{24,0},{1,9},{9,17},{17,25},{25,1},{2,10},{10... | collective-permute-start | bytes 110600 | tf_op jit(solution)/shard_map/ppermute | solution.py:21
  150.0 5.6 %collective-permute-start.27 = (bf16[3,1,3,32,192]{4,2,3,1,0:T(4,128)(2,1)S(1)}, bf16[3,1,3,32,192]{4,2,3,1,0:T(4,128)(2,1)S(1)}, u32[]{:S(2)}, u32[]{:S(2)}) collective-permute-start(bf16[3,1,3,32,192]{4,2,3,1,0:T(4,128)(2,1)S(1)} %pad_maximum_fusion.21), channel_id=1, source_target_pairs={{1,0},{2,1},{3,2},{4,3},{5,4},{6,5},{7,6},{0,7},{9,8},{10,9},{11,1... | collective-permute-start | bytes 331784 | tf_op jit(solution)/shard_map/ppermute | solution.py:23
  150.5 7.3 %collective-permute-start.26 = (bf16[3,1,3,32,192]{4,2,3,1,0:T(4,128)(2,1)S(1)}, bf16[3,1,3,32,192]{4,2,3,1,0:T(4,128)(2,1)S(1)}, u32[]{:S(2)}, u32[]{:S(2)}) collective-permute-start(bf16[3,1,3,32,192]{4,2,3,1,0:T(4,128)(2,1)S(1)} %pad_maximum_fusion.21), channel_id=1, source_target_pairs={{0,1},{1,2},{2,3},{3,4},{4,5},{5,6},{6,7},{7,0},{8,9},{9,10},{10,1... | collective-permute-start | bytes 331784 | tf_op jit(solution)/shard_map/ppermute | solution.py:21
  167.5 4.3 collective-permute-start.29
  168.6 5.2 %collective-permute-start.28 = (bf16[1,1,3,32,192]{4,2,3,1,0:T(4,128)(2,1)S(1)}, bf16[1,1,3,32,192]{4,2,3,1,0:T(4,128)(2,1)S(1)}, u32[]{:S(2)}, u32[]{:S(2)}) collective-permute-start(bf16[1,1,3,32,192]{4,2,3,1,0:T(4,128)(2,1)S(1)} %get-tuple-element.30), channel_id=1, source_target_pairs={{0,8},{8,16},{16,24},{24,0},{1,9},{9,17},{17,25},{25,1},{2,10},{10... | collective-permute-start | bytes 110600 | tf_op jit(solution)/shard_map/ppermute | solution.py:21
  173.9 5.2 %collective-permute-start.31 = (bf16[3,1,3,32,192]{4,2,3,1,0:T(4,128)(2,1)S(1)}, bf16[3,1,3,32,192]{4,2,3,1,0:T(4,128)(2,1)S(1)}, u32[]{:S(2)}, u32[]{:S(2)}) collective-permute-start(bf16[3,1,3,32,192]{4,2,3,1,0:T(4,128)(2,1)S(1)} %pad_maximum_fusion.22), channel_id=1, source_target_pairs={{1,0},{2,1},{3,2},{4,3},{5,4},{6,5},{7,6},{0,7},{9,8},{10,9},{11,1... | collective-permute-start | bytes 331784 | tf_op jit(solution)/shard_map/ppermute | solution.py:23
  174.2 6.9 %collective-permute-start.30 = (bf16[3,1,3,32,192]{4,2,3,1,0:T(4,128)(2,1)S(1)}, bf16[3,1,3,32,192]{4,2,3,1,0:T(4,128)(2,1)S(1)}, u32[]{:S(2)}, u32[]{:S(2)}) collective-permute-start(bf16[3,1,3,32,192]{4,2,3,1,0:T(4,128)(2,1)S(1)} %pad_maximum_fusion.22), channel_id=1, source_target_pairs={{0,1},{1,2},{2,3},{3,4},{4,5},{5,6},{6,7},{7,0},{8,9},{9,10},{10,1... | collective-permute-start | bytes 331784 | tf_op jit(solution)/shard_map/ppermute | solution.py:21
  241.6 5.0 %collective-permute-start.32 = (bf16[1,1,3,32,192]{4,3,2,1,0:T(8,128)(2,1)S(1)}, bf16[1,1,3,32,192]{4,3,2,1,0:T(8,128)(2,1)S(1)}, u32[]{:S(2)}, u32[]{:S(2)}) collective-permute-start(bf16[1,1,3,32,192]{4,3,2,1,0:T(8,128)(2,1)S(1)} %fusion.222), channel_id=1, source_target_pairs={{0,8},{8,16},{16,24},{24,0},{1,9},{9,17},{17,25},{25,1},{2,10},{10... | collective-permute-start | bytes 110600 | tf_op jit(solution)/shard_map/ppermute | solution.py:21
  246.7 6.4 %collective-permute-start.34 = (bf16[3,1,3,32,192]{4,3,2,1,0:T(8,128)(2,1)S(1)}, bf16[3,1,3,32,192]{4,3,2,1,0:T(8,128)(2,1)S(1)}, u32[]{:S(2)}, u32[]{:S(2)}) collective-permute-start(bf16[3,1,3,32,192]{4,3,2,1,0:T(8,128)(2,1)S(1)} %pad_maximum_fusion.24), channel_id=1, source_target_pairs={{0,1},{1,2},{2,3},{3,4},{4,5},{5,6},{6,7},{7,0},{8,9},{9,10},{10,1... | collective-permute-start | bytes 331784 | tf_op jit(solution)/shard_map/ppermute | solution.py:21
  262.5 5.0 %collective-permute-start.36 = (bf16[1,1,3,32,192]{4,3,2,1,0:T(8,128)(2,1)S(1)}, bf16[1,1,3,32,192]{4,3,2,1,0:T(8,128)(2,1)S(1)}, u32[]{:S(2)}, u32[]{:S(2)}) collective-permute-start(bf16[1,1,3,32,192]{4,3,2,1,0:T(8,128)(2,1)S(1)} %fusion.223), channel_id=1, source_target_pairs={{0,8},{8,16},{16,24},{24,0},{1,9},{9,17},{17,25},{25,1},{2,10},{10... | collective-permute-start | bytes 110600 | tf_op jit(solution)/shard_map/ppermute | solution.py:21
  267.7 6.4 %collective-permute-start.38 = (bf16[3,1,3,32,192]{4,3,2,1,0:T(8,128)(2,1)S(1)}, bf16[3,1,3,32,192]{4,3,2,1,0:T(8,128)(2,1)S(1)}, u32[]{:S(2)}, u32[]{:S(2)}) collective-permute-start(bf16[3,1,3,32,192]{4,3,2,1,0:T(8,128)(2,1)S(1)} %pad_maximum_fusion.25), channel_id=1, source_target_pairs={{0,1},{1,2},{2,3},{3,4},{4,5},{5,6},{6,7},{7,0},{8,9},{9,10},{10,1... | collective-permute-start | bytes 331784 | tf_op jit(solution)/shard_map/ppermute | solution.py:21
  284.4 5.0 %collective-permute-start.40 = (bf16[1,1,3,32,192]{4,3,2,1,0:T(8,128)(2,1)S(1)}, bf16[1,1,3,32,192]{4,3,2,1,0:T(8,128)(2,1)S(1)}, u32[]{:S(2)}, u32[]{:S(2)}) collective-permute-start(bf16[1,1,3,32,192]{4,3,2,1,0:T(8,128)(2,1)S(1)} %get-tuple-element.16), channel_id=1, source_target_pairs={{0,8},{8,16},{16,24},{24,0},{1,9},{9,17},{17,25},{25,1},{2,10},{10... | collective-permute-start | bytes 110600 | tf_op jit(solution)/shard_map/ppermute | solution.py:21
  289.5 6.6 %collective-permute-start.42 = (bf16[3,1,3,32,192]{4,3,2,1,0:T(8,128)(2,1)S(1)}, bf16[3,1,3,32,192]{4,3,2,1,0:T(8,128)(2,1)S(1)}, u32[]{:S(2)}, u32[]{:S(2)}) collective-permute-start(bf16[3,1,3,32,192]{4,3,2,1,0:T(8,128)(2,1)S(1)} %pad_maximum_fusion.26), channel_id=1, source_target_pairs={{0,1},{1,2},{2,3},{3,4},{4,5},{5,6},{6,7},{7,0},{8,9},{9,10},{10,1... | collective-permute-start | bytes 331784 | tf_op jit(solution)/shard_map/ppermute | solution.py:21
  305.9 5.0 %collective-permute-start.44 = (bf16[1,1,3,32,192]{4,3,2,1,0:T(8,128)(2,1)S(1)}, bf16[1,1,3,32,192]{4,3,2,1,0:T(8,128)(2,1)S(1)}, u32[]{:S(2)}, u32[]{:S(2)}) collective-permute-start(bf16[1,1,3,32,192]{4,3,2,1,0:T(8,128)(2,1)S(1)} %get-tuple-element.14), channel_id=1, source_target_pairs={{0,8},{8,16},{16,24},{24,0},{1,9},{9,17},{17,25},{25,1},{2,10},{10... | collective-permute-start | bytes 110600 | tf_op jit(solution)/shard_map/ppermute | solution.py:21
  311.1 6.4 %collective-permute-start.46 = (bf16[3,1,3,32,192]{4,3,2,1,0:T(8,128)(2,1)S(1)}, bf16[3,1,3,32,192]{4,3,2,1,0:T(8,128)(2,1)S(1)}, u32[]{:S(2)}, u32[]{:S(2)}) collective-permute-start(bf16[3,1,3,32,192]{4,3,2,1,0:T(8,128)(2,1)S(1)} %pad_maximum_fusion.27), channel_id=1, source_target_pairs={{0,1},{1,2},{2,3},{3,4},{4,5},{5,6},{6,7},{7,0},{8,9},{9,10},{10,1... | collective-permute-start | bytes 331784 | tf_op jit(solution)/shard_map/ppermute | solution.py:21
  328.1 5.0 %collective-permute-start.48 = (bf16[1,1,3,32,192]{4,3,2,1,0:T(8,128)(2,1)S(1)}, bf16[1,1,3,32,192]{4,3,2,1,0:T(8,128)(2,1)S(1)}, u32[]{:S(2)}, u32[]{:S(2)}) collective-permute-start(bf16[1,1,3,32,192]{4,3,2,1,0:T(8,128)(2,1)S(1)} %get-tuple-element.12), channel_id=1, source_target_pairs={{0,8},{8,16},{16,24},{24,0},{1,9},{9,17},{17,25},{25,1},{2,10},{10... | collective-permute-start | bytes 110600 | tf_op jit(solution)/shard_map/ppermute | solution.py:21
  333.2 6.8 %collective-permute-start.50 = (bf16[3,1,3,32,192]{4,3,2,1,0:T(8,128)(2,1)S(1)}, bf16[3,1,3,32,192]{4,3,2,1,0:T(8,128)(2,1)S(1)}, u32[]{:S(2)}, u32[]{:S(2)}) collective-permute-start(bf16[3,1,3,32,192]{4,3,2,1,0:T(8,128)(2,1)S(1)} %pad_maximum_fusion.28), channel_id=1, source_target_pairs={{0,1},{1,2},{2,3},{3,4},{4,5},{5,6},{6,7},{7,0},{8,9},{9,10},{10,1... | collective-permute-start | bytes 331784 | tf_op jit(solution)/shard_map/ppermute | solution.py:21
  349.4 5.0 %collective-permute-start.52 = (bf16[1,1,3,32,192]{4,3,2,1,0:T(8,128)(2,1)S(1)}, bf16[1,1,3,32,192]{4,3,2,1,0:T(8,128)(2,1)S(1)}, u32[]{:S(2)}, u32[]{:S(2)}) collective-permute-start(bf16[1,1,3,32,192]{4,3,2,1,0:T(8,128)(2,1)S(1)} %get-tuple-element.10), channel_id=1, source_target_pairs={{0,8},{8,16},{16,24},{24,0},{1,9},{9,17},{17,25},{25,1},{2,10},{10... | collective-permute-start | bytes 110600 | tf_op jit(solution)/shard_map/ppermute | solution.py:21
  354.5 6.4 %collective-permute-start.54 = (bf16[3,1,3,32,192]{4,3,2,1,0:T(8,128)(2,1)S(1)}, bf16[3,1,3,32,192]{4,3,2,1,0:T(8,128)(2,1)S(1)}, u32[]{:S(2)}, u32[]{:S(2)}) collective-permute-start(bf16[3,1,3,32,192]{4,3,2,1,0:T(8,128)(2,1)S(1)} %pad_maximum_fusion.29), channel_id=1, source_target_pairs={{0,1},{1,2},{2,3},{3,4},{4,5},{5,6},{6,7},{7,0},{8,9},{9,10},{10,1... | collective-permute-start | bytes 331784 | tf_op jit(solution)/shard_map/ppermute | solution.py:21
  371.1 5.0 %collective-permute-start.56 = (bf16[1,1,3,32,192]{4,3,2,1,0:T(8,128)(2,1)S(1)}, bf16[1,1,3,32,192]{4,3,2,1,0:T(8,128)(2,1)S(1)}, u32[]{:S(2)}, u32[]{:S(2)}) collective-permute-start(bf16[1,1,3,32,192]{4,3,2,1,0:T(8,128)(2,1)S(1)} %get-tuple-element.6), channel_id=1, source_target_pairs={{0,8},{8,16},{16,24},{24,0},{1,9},{9,17},{17,25},{25,1},{2,10},{10... | collective-permute-start | bytes 110600 | tf_op jit(solution)/shard_map/ppermute | solution.py:21
  376.2 6.6 %collective-permute-start.58 = (bf16[3,1,3,32,192]{4,3,2,1,0:T(8,128)(2,1)S(1)}, bf16[3,1,3,32,192]{4,3,2,1,0:T(8,128)(2,1)S(1)}, u32[]{:S(2)}, u32[]{:S(2)}) collective-permute-start(bf16[3,1,3,32,192]{4,3,2,1,0:T(8,128)(2,1)S(1)} %pad_maximum_fusion.30), channel_id=1, source_target_pairs={{0,1},{1,2},{2,3},{3,4},{4,5},{5,6},{6,7},{7,0},{8,9},{9,10},{10,1... | collective-permute-start | bytes 331784 | tf_op jit(solution)/shard_map/ppermute | solution.py:21
  392.6 5.0 %collective-permute-start.60 = (bf16[1,1,3,32,192]{4,3,2,1,0:T(8,128)(2,1)S(1)}, bf16[1,1,3,32,192]{4,3,2,1,0:T(8,128)(2,1)S(1)}, u32[]{:S(2)}, u32[]{:S(2)}) collective-permute-start(bf16[1,1,3,32,192]{4,3,2,1,0:T(8,128)(2,1)S(1)} %convert_bitcast_fusion), channel_id=1, source_target_pairs={{0,8},{8,16},{16,24},{24,0},{1,9},{9,17},{17,25},{25,1},{2,10},{10... | collective-permute-start | bytes 110600 | tf_op jit(solution)/shard_map/ppermute | solution.py:21
  397.8 6.4 %collective-permute-start.62 = (bf16[3,1,3,32,192]{4,3,2,1,0:T(8,128)(2,1)S(1)}, bf16[3,1,3,32,192]{4,3,2,1,0:T(8,128)(2,1)S(1)}, u32[]{:S(2)}, u32[]{:S(2)}) collective-permute-start(bf16[3,1,3,32,192]{4,3,2,1,0:T(8,128)(2,1)S(1)} %pad_maximum_fusion.31), channel_id=1, source_target_pairs={{0,1},{1,2},{2,3},{3,4},{4,5},{5,6},{6,7},{7,0},{8,9},{9,10},{10,1... | collective-permute-start | bytes 331784 | tf_op jit(solution)/shard_map/ppermute | solution.py:21
  (18 other events, 78.1 us)
